TPU v7x, 512 devices: a whole 4x4x16 slice. The times are simulated.
512 devices in a mesh: panel: 2 (over x_lo), lat: 8 (over y, core), lon: 32 (over z, x_hi).
Axes of the slice: x: 4 (x_hi: 2, x_lo: 2; x = x_hi * 2 + x_lo), y: 4, z: 16, core: 2. Of those that a mesh axis runs over, the one named last changes fastest.
Arguments:
- fields: float32 [2, 6, 4, 1024, 4096], P('panel', None, None, 'lat', 'lon'), may hold values from -6 to 6
- viscosity: float32 [2, 4, 1024, 4096], P('panel', None, 'lat', 'lon'), may hold values from 0.01 to 0.1
- partner: int32 [2, 8, 1024, 1], P('panel', 'lat', 'lon'), may hold values from 0 to 31; in each aligned block of 32 rows (0 to 31, 32 to 63, ..., all dimensions but the last counted through in order) at most 2 rows name the same one
- src_row: int32 [2, 8, 65536], P('panel', 'lat', 'lon'), may hold values from 0 to 126
- src_col: int32 [2, 8, 65536], P('panel', 'lat', 'lon'), may hold values from 0 to 126
- weight_id: int32 [2, 8, 65536], P('panel', 'lat', 'lon'), may hold values from 0 to 63
- border_angle: float32 [2, 8, 65536], P('panel', 'lat', 'lon'), may hold values from -3.140625 to 3.140625
- dest_cell: int32 [2, 8, 65536], P('panel', 'lat', 'lon'), may hold values from 0 to 16383, as said below
Outputs:
- new_fields: float32 [2, 6, 4, 1024, 4096], P('panel', None, None, 'lat', 'lon')
- pressure: float32 [2, 4, 1024, 4096], P('panel', None, 'lat', 'lon')
Inputs may be any that keep to these rules, and one draw needn't show every extreme that they name: `partner`: A border block's sources lie on the device of the other panel with the same lat index and this lon index; among the 32 blocks of one device no lon index is named by more than 2 blocks. `dest_cell`: the 2048 border cells of one device are distinct cells of its block.
All inputs are finite; a program needn't handle non-finite values.
Results may differ from a plain program's by a relative error of at most 0.0002.
Values sent between devices are 32-bit elements; how exact they have to be, the bound alone decides.
No kernel may reach another device: no remote copies, remote signals or barrier semaphores. Data moves between devices by JAX's collectives and lax.ppermute only.
A program may use at most 128 MiB of HBM per device.

v0:
```python
import math
import jax
import jax.numpy as jnp
from jax import lax
from jax.sharding import PartitionSpec as P

CAP = 2
WQ = 8
BUOYANCY = 0.5


def partner_2(block, axis, apart):
    count = lax.axis_size(axis)
    route = []
    for low in range(count):
        high = low | 1 << apart
        if high != low and high < count:
            route += [(low, high), (high, low)]
    return lax.ppermute(block, axis, route)


def padded_2(shard, sides, width):
    for axis, dim in sides:
        size, length = (lax.axis_size(axis), shard.shape[dim])
        up = [(i, (i + 1) % size) for i in range(size - 1)]
        down = [(j, i) for i, j in up]
        last = lax.slice_in_dim(shard, length - width, length, axis=dim)
        leading = lax.slice_in_dim(shard, 0, width, axis=dim)
        before = lax.ppermute(last, axis, up)
        after = lax.ppermute(leading, axis, down)
        shard = jnp.concatenate([before, shard, after], axis=dim)
    return shard


def metric(row_index, total_rows):
    colatitude = (
        math.pi / 4.0 + (row_index.astype(jnp.float32) + 0.5) * (math.pi / 2.0) / total_rows
    )
    inv_sine = 1.0 / jnp.sin(colatitude)
    return (inv_sine, inv_sine * inv_sine)


def lap_shrink(field, row_gain):
    centre = field[..., 1:-1, 1:-1]
    padded = jnp.pad(centre, [(0, 0)] * (centre.ndim - 3) + [(1, 1), (0, 0), (0, 0)])
    lat_term = field[..., 2:, 1:-1] + field[..., :-2, 1:-1] - 2.0 * centre
    lon_term = field[..., 1:-1, 2:] + field[..., 1:-1, :-2] - 2.0 * centre
    radial = padded[..., 2:, :, :] + padded[..., :-2, :, :] - 2.0 * centre
    return lat_term + row_gain[:, None] * lon_term + radial


def diverge(velocity, inv_sine):
    radial_pad = jnp.pad(velocity[0, :, 1:-1, 1:-1], ((1, 1), (0, 0), (0, 0)))
    lat_part = velocity[1, :, 2:, 1:-1] - velocity[1, :, :-2, 1:-1]
    lon_part = velocity[2, :, 1:-1, 2:] - velocity[2, :, 1:-1, :-2]
    rad_part = radial_pad[2:] - radial_pad[:-2]
    return 0.5 * (lat_part + inv_sine[:, None] * lon_part + rad_part)


def gradient(pressure, inv_sine):
    radial_pad = jnp.pad(pressure[:, 1:-1, 1:-1], ((1, 1), (0, 0), (0, 0)))
    grad_rad = 0.5 * (radial_pad[2:] - radial_pad[:-2])
    grad_lat = 0.5 * (pressure[:, 2:, 1:-1] - pressure[:, :-2, 1:-1])
    grad_lon = 0.5 * inv_sine[:, None] * (pressure[:, 1:-1, 2:] - pressure[:, 1:-1, :-2])
    return (grad_rad, grad_lat, grad_lon)


def cosine_table(length):
    mode_ids = jnp.arange(length, dtype=jnp.float32)
    cell_mid = jnp.arange(length, dtype=jnp.float32) + 0.5
    row_norm = jnp.sqrt(jnp.where(mode_ids > 0, 2.0, 1.0) / length)
    cos_table = row_norm[:, None] * jnp.cos(
        math.pi * mode_ids[:, None] * cell_mid[None, :] / length
    )
    eigenvalue = 4.0 * jnp.sin(math.pi * mode_ids / (2.0 * length)) ** 2
    return (cos_table, eigenvalue)


def coarse_divisor(levels, n_lat, n_lon):
    eig_rad = cosine_table(levels)[1]
    eig_lat = cosine_table(n_lat)[1]
    eig_lon = cosine_table(n_lon)[1]
    return (
        eig_rad[:, None, None]
        + eig_lat[None, :, None]
        + eig_lon[None, None, :]
        + 1.0 / (n_lat * n_lon)
    )


def coarse_solve(block_sum, n_lat, n_lon):
    highest = lax.Precision.HIGHEST
    tab_rad = cosine_table(block_sum.shape[0])[0]
    tab_lat = cosine_table(n_lat)[0]
    tab_lon = cosine_table(n_lon)[0]
    spectrum = jnp.einsum("kr,rlo->klo", tab_rad, block_sum, precision=highest)
    spectrum = jnp.einsum("kl,rlo->rko", tab_lat, spectrum, precision=highest)
    spectrum = jnp.einsum("ko,rlo->rlk", tab_lon, spectrum, precision=highest)
    spectrum = spectrum / coarse_divisor(block_sum.shape[0], n_lat, n_lon)
    restored = jnp.einsum("kr,klo->rlo", tab_rad, spectrum, precision=highest)
    restored = jnp.einsum("kl,rko->rlo", tab_lat, restored, precision=highest)
    restored = jnp.einsum("ko,rlk->rlo", tab_lon, restored, precision=highest)
    return restored / math.sqrt(n_lat * n_lon)


def fractions(weight_ids):
    frac_lat = ((weight_ids // WQ).astype(jnp.float32) + 0.5) / WQ
    frac_lon = ((weight_ids % WQ).astype(jnp.float32) + 0.5) / WQ
    return (frac_lat, frac_lon)


def bilinear(lower_left, lower_right, upper_left, upper_right, frac_lat, frac_lon):
    return (
        (1.0 - frac_lat) * (1.0 - frac_lon) * lower_left
        + (1.0 - frac_lat) * frac_lon * lower_right
        + frac_lat * (1.0 - frac_lon) * upper_left
        + frac_lat * frac_lon * upper_right
    )


def shards(fields, viscosity, partner, src_row, src_col, weight_id, border_angle, dest_cell):
    n_lat = lax.axis_size("lat")
    n_lon = lax.axis_size("lon")
    lat_pos = lax.axis_index("lat")
    lon_pos = lax.axis_index("lon")
    own_fields = fields[0]
    levels, rows_dev, cols_dev = (own_fields.shape[1], own_fields.shape[2], own_fields.shape[3])
    channels = 6 * levels
    blocks = partner.shape[2]
    block_cells = src_row.shape[2] // blocks
    capacity = CAP
    slot_count = n_lon * capacity
    total_rows = rows_dev * n_lat
    flat_cells = own_fields.reshape(channels, rows_dev * cols_dev)
    target = partner[0, 0, :, 0]
    onehot = (target[:, None] == jnp.arange(n_lon, dtype=jnp.int32)[None, :]).astype(jnp.int32)
    before = jnp.sum(
        (jnp.cumsum(onehot, axis=0, dtype=jnp.int32) - onehot) * onehot, axis=1, dtype=jnp.int32
    )
    slot_of = target * capacity + before
    base_cell = (src_row[0, 0] * cols_dev + src_col[0, 0]).reshape(blocks, block_cells)
    weight_ids = weight_id[0, 0].reshape(blocks, block_cells)
    empty = jnp.zeros((slot_count, block_cells), jnp.int32)
    requests = partner_2(
        empty.at[slot_of].set(base_cell).reshape(n_lon, capacity * block_cells), "panel", 0
    )
    requests = lax.all_to_all(requests, "lon", split_axis=0, concat_axis=0, tiled=True)
    served = jnp.stack(
        tuple(
            (
                jnp.take(flat_cells, requests + offset, axis=1)
                for offset in (0, 1, cols_dev, cols_dev + 1)
            )
        ),
        axis=0,
    )
    served = lax.all_to_all(served, "lon", split_axis=2, concat_axis=2, tiled=True)
    served = partner_2(served, "panel", 0)
    picked = served.reshape(4, channels, slot_count, block_cells)[:, :, slot_of, :]
    frac_lat, frac_lon = fractions(weight_ids)
    values = bilinear(picked[0], picked[1], picked[2], picked[3], frac_lat, frac_lon)
    values = values.reshape(6, levels, blocks * block_cells)
    turn = border_angle[0, 0]
    cos_angle = jnp.cos(turn)
    sin_angle = jnp.sin(turn)
    rotated = jnp.stack(
        [
            values[0],
            cos_angle * values[1] + sin_angle * values[2],
            cos_angle * values[2] - sin_angle * values[1],
            values[3],
            cos_angle * values[4] + sin_angle * values[5],
            cos_angle * values[5] - sin_angle * values[4],
        ],
        axis=0,
    ).reshape(channels, blocks * block_cells)
    filled = flat_cells.at[:, dest_cell[0, 0]].set(rotated).reshape(6, levels, rows_dev, cols_dev)
    diffusivity = viscosity[0]
    inv_own, gain_own = metric(
        lat_pos * rows_dev + jnp.arange(-0, rows_dev + 0, dtype=jnp.int32), total_rows
    )
    widened = padded_2(filled, (("lat", 2), ("lon", 3)), 1)
    stepped = filled + diffusivity[None] * lap_shrink(widened, gain_own)
    stepped = jnp.concatenate([stepped[0:1] + BUOYANCY * filled[3:4], stepped[1:]], axis=0)
    velocity = padded_2(stepped[0:3], (("lat", 2), ("lon", 3)), 1)
    divergence = diverge(velocity, inv_own)
    press_one = -divergence / (4.0 + 2.0 * gain_own)[:, None]
    press_wide = padded_2(press_one, (("lat", 1), ("lon", 2)), 1)
    resid_one = -divergence + lap_shrink(press_wide, gain_own)
    block_sum = jnp.sum(resid_one, axis=(1, 2)) * (1.0 / math.sqrt(rows_dev * cols_dev))
    gathered = lax.all_gather(block_sum[:, None], ("lat", "lon"), axis=1, tiled=True)
    coarse = coarse_solve(gathered.reshape(levels, n_lat, n_lon), n_lat, n_lon)
    start = jnp.zeros((), jnp.int32)
    own_coarse = lax.dynamic_slice(coarse, (start, lat_pos, lon_pos), (levels, 1, 1)).reshape(
        levels
    )
    pressure = press_one + own_coarse[:, None, None]
    press_rim = padded_2(pressure, (("lat", 1), ("lon", 2)), 1)
    grad_rad, grad_lat, grad_lon = gradient(press_rim, inv_own)
    result = jnp.stack(
        [
            stepped[0] - grad_rad,
            stepped[1] - grad_lat,
            stepped[2] - grad_lon,
            stepped[3],
            stepped[4],
            stepped[5],
        ],
        axis=0,
    )
    return (result[None], pressure[None])


def solution(mesh):
    return jax.shard_map(
        shards,
        mesh=mesh,
        in_specs=(
            P("panel", None, None, "lat", "lon"),
            P("panel", None, "lat", "lon"),
            P("panel", "lat", "lon", None),
            P("panel", "lat", "lon"),
            P("panel", "lat", "lon"),
            P("panel", "lat", "lon"),
            P("panel", "lat", "lon"),
            P("panel", "lat", "lon"),
        ),
        out_specs=(P("panel", None, None, "lat", "lon"), P("panel", None, "lat", "lon")),
        check_vma=False,
    )
```

profile of v0, /device:TPU:32, one launch (start us, length us, event | category | flops | bytes accessed | tf_op | source)
XLA Modules:
  0.0 1006.0 jit_solution(13711686433813685990)
XLA Ops:
  4.5 3.4 collective-permute-start
  10.2 17.8 %all-to-all-start = ((s32[32,1,128]{2,1,0:T(1,128)}), s32[32,1,128]{2,1,0:T(1,128)S(1)}, u32[]{:S(2)}, u32[]{:S(2)}) async-start(s32[32,1,128]{2,1,0:T(1,128)} %bitcast.6), calls=%async_computation | async-start | bytes 32768 | tf_op jit(solution)/shard_map/all_to_all | solution.py:147
  30.4 4.7 copy.95
  35.0 6.4 all-to-all-done
  41.5 14.1 %gather_fusion.1 = f32[4096,24]{1,0:T(8,128)S(1)} fusion(f32[24,16384]{0,1:T(8,128)} %copy.95, s32[4096]{0:T(1024)S(1)} %get-tuple-element.38), kind=kCustom, calls=%fused_computation.clone | custom fusion | bytes 802816 | tf_op jit(solution)/shard_map/jit(_take)/gather | solution.py:151
  56.2 14.1 %gather_fusion.2 = f32[4096,24]{1,0:T(8,128)S(1)} fusion(f32[24,16384]{0,1:T(8,128)} %copy.95, s32[4096]{0:T(1024)S(1)} %get-tuple-element.39), kind=kCustom, calls=%fused_computation.1.clone | custom fusion | bytes 802816 | tf_op jit(solution)/shard_map/jit(_take)/gather | solution.py:151
  71.0 14.1 %gather_fusion.3 = f32[4096,24]{1,0:T(8,128)S(1)} fusion(f32[24,16384]{0,1:T(8,128)} %copy.95, s32[4096]{0:T(1024)S(1)} %get-tuple-element.40), kind=kCustom, calls=%fused_computation.2.clone | custom fusion | bytes 802816 | tf_op jit(solution)/shard_map/jit(_take)/gather | solution.py:151
  85.7 14.1 %gather_fusion.4 = f32[4096,24]{1,0:T(8,128)S(1)} fusion(f32[24,16384]{0,1:T(8,128)} %copy.95, s32[4096]{0:T(1024)S(1)} %get-tuple-element.41), kind=kCustom, calls=%fused_computation.3.clone | custom fusion | bytes 802816 | tf_op jit(solution)/shard_map/jit(_take)/gather | solution.py:151
  103.5 8.3 all-to-all-start.1
  111.9 73.8 %all-to-all-done.1 = f32[4,24,32,128]{3,1,0,2:T(8,128)S(1)} async-done(((f32[4,24,32,128]{3,1,0,2:T(8,128)}), f32[4,24,32,128]{3,1,0,2:T(8,128)S(1)}, u32[]{:S(2)}, u32[]{:S(2)}) %all-to-all-start.1) | async-done | bytes 1572896 | tf_op jit(solution)/shard_map/all_to_all | solution.py:157
  190.0 26.9 %collective-permute-done.1 = f32[4,24,32,128]{3,1,0,2:T(8,128)S(1)} collective-permute-done((f32[4,24,32,128]{3,1,0,2:T(8,128)S(1)}, f32[4,24,32,128]{3,1,0,2:T(8,128)S(1)}, u32[]{:S(2)}, u32[]{:S(2)}) %collective-permute-start.1) | collective-permute-done | bytes 1572896 | tf_op jit(solution)/shard_map/ppermute | solution.py:19
  221.4 3.5 copy.85
  224.9 2.5 gather_fusion
  228.9 12.2 %scatter_fusion = f32[24,16384]{0,1:T(8,128)} fusion(f32[24,16384]{0,1:T(8,128)} %copy.95, s32[2048]{0:T(1024)S(1)} %bitcast.183, f32[2048,24]{1,0:T(8,128)S(1)} %copy.96), kind=kCustom, calls=%fused_computation.6 | custom fusion | bytes 598016 | tf_op jit(solution)/shard_map/scatter | solution.py:177
  241.1 5.1 copy.97
  247.8 3.0 collective-permute-start.3
  256.4 7.6 collective-permute-start.5
  266.4 4.8 collective-permute-start.4
  271.2 6.6 slice_multiply_fusion
  277.8 5.2 copy.102
  286.6 3.5 fusion.4
  291.6 3.4 collective-permute-start.7
  299.0 5.1 collective-permute-start.8
  309.2 4.5 collective-permute-done.9
  317.7 3.9 collective-permute-start.11
  325.6 4.9 collective-permute-start.13
  330.5 9.0 collective-permute-done.12
  340.0 638.4 %all-gather = f32[256,1,4]{2,1,0:T(1,128)S(1)} all-gather(f32[1,1,4]{2,1,0:T(1,128)S(1)} %multiply_bitcast_fusion), channel_id=1, replica_groups=mesh['panel'=2,'lat'=8,'lon'=32] {'lat','lon'}, dimensions={0}, use_global_device_ids=true | all-gather | bytes 4112 | tf_op jit(solution)/shard_map/all_gather | solution.py:191
  982.1 3.0 collective-permute-start.15
  986.1 2.6 collective-permute-start.16
  988.8 4.7 collective-permute-start.17
  994.3 10.1 %collective-permute-done.16 = f32[4,130,1]{2,1,0:T(8,128)S(1)} collective-permute-done((f32[4,130,1]{2,1,0:T(8,128)S(1)}, f32[4,130,1]{2,1,0:T(8,128)S(1)}, u32[]{:S(2)}, u32[]{:S(2)}) %collective-permute-start.16) | collective-permute-done | bytes 2112 | tf_op jit(solution)/shard_map/ppermute | solution.py:30
  (129 shorter events, 63.0 us)
Async XLA Ops:
  4.5 5.7 collective-permute-start
  10.2 31.2 %all-to-all-start = ((s32[32,1,128]{2,1,0:T(1,128)}), s32[32,1,128]{2,1,0:T(1,128)S(1)}, u32[]{:S(2)}, u32[]{:S(2)}) async-start(s32[32,1,128]{2,1,0:T(1,128)} %bitcast.6), calls=%async_computation | async-start | bytes 32768 | tf_op jit(solution)/shard_map/all_to_all | solution.py:147
  101.2 1.0 copy-start
  103.5 85.3 %copy-start.2 = (s32[1,1,2048]{2,1,0:T(1,128)S(1)}, s32[1,1,2048]{2,1,0:T(1,128)}, u32[]{:S(2)}) copy-start(s32[1,1,2048]{2,1,0:T(1,128)} %param.15) | copy-start | bytes 24580
  103.5 86.2 %copy-start.3 = (s32[1,1,2048]{2,1,0:T(1,128)S(1)}, s32[1,1,2048]{2,1,0:T(1,128)}, u32[]{:S(2)}) copy-start(s32[1,1,2048]{2,1,0:T(1,128)} %param.17) | copy-start | bytes 24580
  103.5 86.3 %copy-start.1 = (f32[1,1,2048]{2,1,0:T(1,128)S(1)}, f32[1,1,2048]{2,1,0:T(1,128)}, u32[]{:S(2)}) copy-start(f32[1,1,2048]{2,1,0:T(1,128)} %param.16) | copy-start | bytes 24580
  103.5 82.3 %all-to-all-start.1 = ((f32[4,24,32,128]{3,1,0,2:T(8,128)}), f32[4,24,32,128]{3,1,0,2:T(8,128)S(1)}, u32[]{:S(2)}, u32[]{:S(2)}) async-start(f32[4,24,32,128]{3,1,0,2:T(8,128)} %pad_maximum_fusion.9), calls=%async_computation.1 | async-start | bytes 3145728 | tf_op jit(solution)/shard_map/all_to_all | solution.py:157
  185.8 31.2 %collective-permute-start.1 = (f32[4,24,32,128]{3,1,0,2:T(8,128)S(1)}, f32[4,24,32,128]{3,1,0,2:T(8,128)S(1)}, u32[]{:S(2)}, u32[]{:S(2)}) collective-permute-start(f32[4,24,32,128]{3,1,0,2:T(8,128)S(1)} %all-to-all-done.1), channel_id=1, source_target_pairs={{0,256},{256,0},{1,257},{257,1},{2,258},{258,2},{3,259},{259,3},{4... | collective-permute-start | bytes 4718600 | tf_op jit(solution)/shard_map/ppermute | solution.py:19
  246.5 4.4 collective-permute-start.2
  247.8 3.9 collective-permute-start.3
  256.4 26.6 %collective-permute-start.5 = (f32[6,4,130,1]{2,1,3,0:T(4,128)S(1)}, f32[6,4,130,1]{2,1,3,0:T(4,128)S(1)}, u32[]{:S(2)}, u32[]{:S(2)}) collective-permute-start(f32[6,4,130,1]{2,1,3,0:T(4,128)S(1)} %copy.100), channel_id=1, source_target_pairs={{0,1},{1,2},{2,3},{3,4},{4,5},{5,6},{6,7},{7,8},{8,9},{9,10},{10,1... | collective-permute-start | bytes 37448 | tf_op jit(solution)/shard_map/ppermute | solution.py:29
  266.4 18.4 %collective-permute-start.4 = (f32[6,4,130,1]{2,1,3,0:T(4,128)S(1)}, f32[6,4,130,1]{2,1,3,0:T(4,128)S(1)}, u32[]{:S(2)}, u32[]{:S(2)}) collective-permute-start(f32[6,4,130,1]{2,1,3,0:T(4,128)S(1)} %copy.98), channel_id=1, source_target_pairs={{1,0},{2,1},{3,2},{4,3},{5,4},{6,5},{7,6},{8,7},{9,8},{10,9},{11,1... | collective-permute-start | bytes 37448 | tf_op jit(solution)/shard_map/ppermute | solution.py:30
  290.3 4.8 collective-permute-start.6
  291.6 4.3 collective-permute-start.7
  299.0 9.0 collective-permute-start.8
  305.7 8.0 collective-permute-start.9
  316.4 5.2 collective-permute-start.10
  317.7 4.7 collective-permute-start.11
  323.2 16.4 %collective-permute-start.12 = (f32[4,130,1]{2,1,0:T(8,128)}, f32[4,130,1]{2,1,0:T(8,128)S(1)}, u32[]{:S(2)}, u32[]{:S(2)}) collective-permute-start(f32[4,130,1]{2,1,0:T(8,128)} %get-tuple-element.23), channel_id=1, source_target_pairs={{1,0},{2,1},{3,2},{4,3},{5,4},{6,5},{7,6},{8,7},{9,8},{10,9},{11,1... | collective-permute-start | bytes 6248 | tf_op jit(solution)/shard_map/ppermute | solution.py:30
  325.6 14.0 %collective-permute-start.13 = (f32[4,130,1]{2,1,0:T(8,128)S(1)}, f32[4,130,1]{2,1,0:T(8,128)S(1)}, u32[]{:S(2)}, u32[]{:S(2)}) collective-permute-start(f32[4,130,1]{2,1,0:T(8,128)S(1)} %get-tuple-element.24), channel_id=1, source_target_pairs={{0,1},{1,2},{2,3},{3,4},{4,5},{5,6},{6,7},{7,8},{8,9},{9,10},{10,1... | collective-permute-start | bytes 6248 | tf_op jit(solution)/shard_map/ppermute | solution.py:29
  980.8 4.5 collective-permute-start.14
  982.1 3.8 collective-permute-start.15
  986.1 18.3 %collective-permute-start.16 = (f32[4,130,1]{2,1,0:T(8,128)S(1)}, f32[4,130,1]{2,1,0:T(8,128)S(1)}, u32[]{:S(2)}, u32[]{:S(2)}) collective-permute-start(f32[4,130,1]{2,1,0:T(8,128)S(1)} %get-tuple-element.21), channel_id=1, source_target_pairs={{1,0},{2,1},{3,2},{4,3},{5,4},{6,5},{7,6},{8,7},{9,8},{10,9},{11,1... | collective-permute-start | bytes 6248 | tf_op jit(solution)/shard_map/ppermute | solution.py:30
  988.8 15.6 %collective-permute-start.17 = (f32[4,130,1]{2,1,0:T(8,128)S(1)}, f32[4,130,1]{2,1,0:T(8,128)S(1)}, u32[]{:S(2)}, u32[]{:S(2)}) collective-permute-start(f32[4,130,1]{2,1,0:T(8,128)S(1)} %get-tuple-element.22), channel_id=1, source_target_pairs={{0,1},{1,2},{2,3},{3,4},{4,5},{5,6},{6,7},{7,8},{8,9},{9,10},{10,1... | collective-permute-start | bytes 6248 | tf_op jit(solution)/shard_map/ppermute | solution.py:29
where the time goes:
time: 1010 us
  blocking collectives  638 us (63%)
  waiting for transfers between devices  136 us (13%)
  local copies, waits for them, and re-layouts  122 us (12%)
  starting transfers between devices  85 us (8%)
  other arithmetic  20.7 us (2%)
    all_gather x1, blocking collectives, shards(): lax.all_gather(block_sum[:, None], ('lat', 'lon'), axis=1, tiled=True)  638 us
    all_to_all x1, waiting for transfers between devices, shards(): lax.all_to_all(served, 'lon', split_axis=2, concat_axis=2, tiled=True)  73.8 us
    gather x8, local copies, waits for them, and re-layouts, shards(): jnp.take(flat_cells, requests + offset, axis=1)  59.6 us
    ppermute x8, starting transfers between devices, padded_2(): before = lax.ppermute(last, axis, up)  32.9 us
    ppermute x2, waiting for transfers between devices, partner_2(): return lax.ppermute(block, axis, route)  29.2 us
  transfers between devices with their start and end apart: 20, of which 11 were waited for; matrix products, arithmetic and copies ran while one was open for 3% of the time, Pallas kernels for 0%

commit v1 on v0

--- a/solution.py
+++ b/solution.py
@@ -188,7 +188,12 @@
     press_wide = padded_2(press_one, (("lat", 1), ("lon", 2)), 1)
     resid_one = -divergence + lap_shrink(press_wide, gain_own)
     block_sum = jnp.sum(resid_one, axis=(1, 2)) * (1.0 / math.sqrt(rows_dev * cols_dev))
-    gathered = lax.all_gather(block_sum[:, None], ("lat", "lon"), axis=1, tiled=True)
+    gathered = jnp.concatenate(
+        lax.all_to_all(
+            jnp.stack([block_sum[:, None]] * lax.axis_size(("lat", "lon"))), ("lat", "lon"), 0, 0
+        ),
+        axis=1,
+    )
     coarse = coarse_solve(gathered.reshape(levels, n_lat, n_lon), n_lat, n_lon)
     start = jnp.zeros((), jnp.int32)
     own_coarse = lax.dynamic_slice(coarse, (start, lat_pos, lon_pos), (levels, 1, 1)).reshape(

time: 1010 us -> 406 us (0.40)
  blocking collectives: 638 us -> 0 us
  starting transfers between devices: 85 us -> 104 us
  waiting for transfers between devices: 136 us -> 153 us
    all_gather x1 -> x0, blocking collectives: 638 us -> none  [shards(): lax.all_gather(block_sum[:, None], ('lat', 'lon'), axis=1, tiled=True)]
    all_to_all x0 -> x1, starting transfers between devices: none -> 19.3 us  [shards(): lax.all_to_all(jnp.stack([block_sum[:, None]] * lax.axis_size(('lat', 'lo...]
    all_to_all x0 -> x1, waiting for transfers between devices: none -> 19.2 us  [shards(): lax.all_to_all(jnp.stack([block_sum[:, None]] * lax.axis_size(('lat', 'lo...]
  transfers between devices with their start and end apart: 20 -> 21, of which waited for: 11 -> 13; matrix products, arithmetic and copies ran while one was open for 3% -> 7% of each run, Pallas kernels for 0% -> 0%
where the time goes in v1:
time: 406 us; the launch traced here: 404 us
  waiting for transfers between devices  153 us (38%)
  local copies, waits for them, and re-layouts  122 us (30%)
  starting transfers between devices  104 us (26%)
  other arithmetic  20.8 us (5%)
    all_to_all x1, waiting for transfers between devices, shards(): lax.all_to_all(served, 'lon', split_axis=2, concat_axis=2, tiled=True)  73.9 us
    gather x8, local copies, waits for them, and re-layouts, shards(): jnp.take(flat_cells, requests + offset, axis=1)  59.6 us
    ppermute x8, starting transfers between devices, padded_2(): before = lax.ppermute(last, axis, up)  31.9 us
    ppermute x2, waiting for transfers between devices, partner_2(): return lax.ppermute(block, axis, route)  29.2 us
    ppermute x8, starting transfers between devices, padded_2(): after = lax.ppermute(leading, axis, down)  21.2 us
    all_to_all x1, starting transfers between devices, shards(): lax.all_to_all(jnp.stack([block_sum[:, None]] * lax.axis_size(('lat', 'lo...  19.3 us
    all_to_all x1, waiting for transfers between devices, shards(): lax.all_to_all(jnp.stack([block_sum[:, None]] * lax.axis_size(('lat', 'lo...  19.2 us
    all_to_all x1, starting transfers between devices, shards(): lax.all_to_all(requests, 'lon', split_axis=0, concat_axis=0, tiled=True)  17.8 us
  transfers between devices with their start and end apart: 21, of which 13 were waited for; matrix products, arithmetic and copies ran while one was open for 7% of the time, Pallas kernels for 0%

profile of v1, /device:TPU:32, one launch (start us, length us, event | category | flops | bytes accessed | tf_op | source)
XLA Modules:
  0.0 404.2 jit_solution(4699220876035040230)
XLA Ops:
  4.5 3.4 collective-permute-start
  10.2 17.8 %all-to-all-start = ((s32[32,1,128]{2,1,0:T(1,128)}), s32[32,1,128]{2,1,0:T(1,128)S(1)}, u32[]{:S(2)}, u32[]{:S(2)}) async-start(s32[32,1,128]{2,1,0:T(1,128)} %bitcast.6), calls=%async_computation | async-start | bytes 32768 | tf_op jit(solution)/shard_map/all_to_all | solution.py:147
  30.4 4.7 %copy.95 = f32[24,16384]{0,1:T(8,128)} copy(f32[24,16384]{1,0:T(8,128)S(1)} %bitcast.158) | data formatting | bytes 3145728 | tf_op jit(solution)/shard_map/reshape;squeeze | solution.py:134
  35.1 6.4 %all-to-all-done = s32[32,1,128]{2,1,0:T(1,128)S(1)} async-done(((s32[32,1,128]{2,1,0:T(1,128)}), s32[32,1,128]{2,1,0:T(1,128)S(1)}, u32[]{:S(2)}, u32[]{:S(2)}) %all-to-all-start) | async-done | bytes 16416 | tf_op jit(solution)/shard_map/all_to_all | solution.py:147
  41.5 14.1 %gather_fusion.1 = f32[4096,24]{1,0:T(8,128)S(1)} fusion(f32[24,16384]{0,1:T(8,128)} %copy.95, s32[4096]{0:T(1024)S(1)} %get-tuple-element.38), kind=kCustom, calls=%fused_computation.clone | custom fusion | bytes 802816 | tf_op jit(solution)/shard_map/jit(_take)/gather | solution.py:151
  56.2 14.1 %gather_fusion.2 = f32[4096,24]{1,0:T(8,128)S(1)} fusion(f32[24,16384]{0,1:T(8,128)} %copy.95, s32[4096]{0:T(1024)S(1)} %get-tuple-element.39), kind=kCustom, calls=%fused_computation.1.clone | custom fusion | bytes 802816 | tf_op jit(solution)/shard_map/jit(_take)/gather | solution.py:151
  70.9 14.1 %gather_fusion.3 = f32[4096,24]{1,0:T(8,128)S(1)} fusion(f32[24,16384]{0,1:T(8,128)} %copy.95, s32[4096]{0:T(1024)S(1)} %get-tuple-element.40), kind=kCustom, calls=%fused_computation.2.clone | custom fusion | bytes 802816 | tf_op jit(solution)/shard_map/jit(_take)/gather | solution.py:151
  85.7 14.1 %gather_fusion.4 = f32[4096,24]{1,0:T(8,128)S(1)} fusion(f32[24,16384]{0,1:T(8,128)} %copy.95, s32[4096]{0:T(1024)S(1)} %get-tuple-element.41), kind=kCustom, calls=%fused_computation.3.clone | custom fusion | bytes 802816 | tf_op jit(solution)/shard_map/jit(_take)/gather | solution.py:151
  103.5 8.3 %all-to-all-start.1 = ((f32[4,24,32,128]{3,1,0,2:T(8,128)}), f32[4,24,32,128]{3,1,0,2:T(8,128)S(1)}, u32[]{:S(2)}, u32[]{:S(2)}) async-start(f32[4,24,32,128]{3,1,0,2:T(8,128)} %pad_maximum_fusion.9), calls=%async_computation.1 | async-start | bytes 3145728 | tf_op jit(solution)/shard_map/all_to_all | solution.py:157
  111.9 73.9 %all-to-all-done.1 = f32[4,24,32,128]{3,1,0,2:T(8,128)S(1)} async-done(((f32[4,24,32,128]{3,1,0,2:T(8,128)}), f32[4,24,32,128]{3,1,0,2:T(8,128)S(1)}, u32[]{:S(2)}, u32[]{:S(2)}) %all-to-all-start.1) | async-done | bytes 1572896 | tf_op jit(solution)/shard_map/all_to_all | solution.py:157
  190.0 26.9 %collective-permute-done.1 = f32[4,24,32,128]{3,1,0,2:T(8,128)S(1)} collective-permute-done((f32[4,24,32,128]{3,1,0,2:T(8,128)S(1)}, f32[4,24,32,128]{3,1,0,2:T(8,128)S(1)}, u32[]{:S(2)}, u32[]{:S(2)}) %collective-permute-start.1) | collective-permute-done | bytes 1572896 | tf_op jit(solution)/shard_map/ppermute | solution.py:19
  221.4 3.5 copy.85
  228.9 12.2 %scatter_fusion = f32[24,16384]{0,1:T(8,128)} fusion(f32[24,16384]{0,1:T(8,128)} %copy.95, s32[2048]{0:T(1024)S(1)} %bitcast.179, f32[2048,24]{1,0:T(8,128)S(1)} %copy.96), kind=kCustom, calls=%fused_computation.6 | custom fusion | bytes 598016 | tf_op jit(solution)/shard_map/scatter | solution.py:177
  241.1 5.1 %copy.97 = f32[24,16384]{1,0:T(8,128)S(1)} copy(f32[24,16384]{0,1:T(8,128)} %scatter_fusion) | data formatting | bytes 3145728 | tf_op jit(solution)/shard_map/scatter | solution.py:177
  247.8 3.0 collective-permute-start.3
  256.4 7.6 %collective-permute-start.5 = (f32[6,4,130,1]{2,1,3,0:T(4,128)S(1)}, f32[6,4,130,1]{2,1,3,0:T(4,128)S(1)}, u32[]{:S(2)}, u32[]{:S(2)}) collective-permute-start(f32[6,4,130,1]{2,1,3,0:T(4,128)S(1)} %copy.100), channel_id=1, source_target_pairs={{0,1},{1,2},{2,3},{3,4},{4,5},{5,6},{6,7},{7,8},{8,9},{9,10},{10,1... | collective-permute-start | bytes 37448 | tf_op jit(solution)/shard_map/ppermute | solution.py:29
  266.4 4.8 %collective-permute-start.4 = (f32[6,4,130,1]{2,1,3,0:T(4,128)S(1)}, f32[6,4,130,1]{2,1,3,0:T(4,128)S(1)}, u32[]{:S(2)}, u32[]{:S(2)}) collective-permute-start(f32[6,4,130,1]{2,1,3,0:T(4,128)S(1)} %copy.98), channel_id=1, source_target_pairs={{1,0},{2,1},{3,2},{4,3},{5,4},{6,5},{7,6},{8,7},{9,8},{10,9},{11,1... | collective-permute-start | bytes 37448 | tf_op jit(solution)/shard_map/ppermute | solution.py:30
  271.2 6.6 %slice_multiply_fusion = f32[4,16384]{0,1:T(8,128)} fusion(f32[24,16384]{0,1:T(8,128)} %scatter_fusion), kind=kLoop, calls=%fused_computation.7 | loop fusion | flops 65536 | bytes 524288 | tf_op jit(solution)/shard_map/mul | solution.py:184
  277.8 5.2 %copy.102 = f32[1,4,128,128]{3,2,1,0:T(8,128)S(1)} copy(f32[1,4,128,128]{1,3,2,0:T(8,128)} %bitcast.153) | data formatting | bytes 524288 | tf_op jit(solution)/shard_map/mul | solution.py:184
  286.6 3.5 fusion.4
  291.6 3.4 collective-permute-start.7
  299.0 5.1 %collective-permute-start.8 = (f32[3,4,130,1]{2,1,3,0:T(4,128)S(1)}, f32[3,4,130,1]{2,1,3,0:T(4,128)S(1)}, u32[]{:S(2)}, u32[]{:S(2)}) collective-permute-start(f32[3,4,130,1]{2,1,3,0:T(4,128)S(1)} %copy.103), channel_id=1, source_target_pairs={{1,0},{2,1},{3,2},{4,3},{5,4},{6,5},{7,6},{8,7},{9,8},{10,9},{11,1... | collective-permute-start | bytes 18728 | tf_op jit(solution)/shard_map/ppermute | solution.py:30
  309.3 4.5 %collective-permute-done.9 = f32[3,4,130,1]{2,1,3,0:T(4,128)S(1)} collective-permute-done((f32[3,4,130,1]{2,1,3,0:T(4,128)S(1)}, f32[3,4,130,1]{2,1,3,0:T(4,128)S(1)}, u32[]{:S(2)}, u32[]{:S(2)}) %collective-permute-start.9) | collective-permute-done | bytes 6272 | tf_op jit(solution)/shard_map/ppermute | solution.py:29
  317.7 3.9 collective-permute-start.11
  325.0 4.9 %collective-permute-start.13 = (f32[4,130,1]{2,1,0:T(8,128)S(1)}, f32[4,130,1]{2,1,0:T(8,128)S(1)}, u32[]{:S(2)}, u32[]{:S(2)}) collective-permute-start(f32[4,130,1]{2,1,0:T(8,128)S(1)} %get-tuple-element.24), channel_id=1, source_target_pairs={{0,1},{1,2},{2,3},{3,4},{4,5},{5,6},{6,7},{7,8},{8,9},{9,10},{10,1... | collective-permute-start | bytes 6248 | tf_op jit(solution)/shard_map/ppermute | solution.py:29
  332.8 4.1 %collective-permute-done.13 = f32[4,130,1]{2,1,0:T(8,128)S(1)} collective-permute-done((f32[4,130,1]{2,1,0:T(8,128)S(1)}, f32[4,130,1]{2,1,0:T(8,128)S(1)}, u32[]{:S(2)}, u32[]{:S(2)}) %collective-permute-start.13) | collective-permute-done | bytes 2112 | tf_op jit(solution)/shard_map/ppermute | solution.py:29
  337.9 19.3 %all-to-all-start.2 = ((f32[256,4,1]{1,2,0:T(1,128)}), f32[256,4,1]{1,2,0:T(1,128)S(1)}, u32[]{:S(2)}, u32[]{:S(2)}) async-start(f32[256,4,1]{1,2,0:T(1,128)} %stack.44), calls=%async_computation.2 | async-start | bytes 262144 | tf_op jit(solution)/shard_map/all_to_all | solution.py:192
  357.3 19.2 %all-to-all-done.2 = f32[256,4,1]{1,2,0:T(1,128)S(1)} async-done(((f32[256,4,1]{1,2,0:T(1,128)}), f32[256,4,1]{1,2,0:T(1,128)S(1)}, u32[]{:S(2)}, u32[]{:S(2)}) %all-to-all-start.2) | async-done | bytes 4128 | tf_op jit(solution)/shard_map/all_to_all | solution.py:192
  380.3 3.1 collective-permute-start.15
  384.3 3.7 collective-permute-start.16
  388.0 3.7 collective-permute-start.17
  392.5 10.1 %collective-permute-done.16 = f32[4,130,1]{2,1,0:T(8,128)S(1)} collective-permute-done((f32[4,130,1]{2,1,0:T(8,128)S(1)}, f32[4,130,1]{2,1,0:T(8,128)S(1)}, u32[]{:S(2)}, u32[]{:S(2)}) %collective-permute-start.16) | collective-permute-done | bytes 2112 | tf_op jit(solution)/shard_map/ppermute | solution.py:30
  (131 shorter events, 68.5 us)
Async XLA Ops:
  4.5 5.7 %collective-permute-start = (s32[32,128]{1,0:T(8,128)S(1)}, s32[32,128]{1,0:T(8,128)}, u32[]{:S(2)}, u32[]{:S(2)}) collective-permute-start(s32[32,128]{1,0:T(8,128)S(1)} %reshape.634), channel_id=1, source_target_pairs={{0,256},{256,0},{1,257},{257,1},{2,258},{258,2},{3,259},{259,3},{4... | collective-permute-start | bytes 49160 | tf_op jit(solution)/shard_map/ppermute | solution.py:19
  10.2 31.2 %all-to-all-start = ((s32[32,1,128]{2,1,0:T(1,128)}), s32[32,1,128]{2,1,0:T(1,128)S(1)}, u32[]{:S(2)}, u32[]{:S(2)}) async-start(s32[32,1,128]{2,1,0:T(1,128)} %bitcast.6), calls=%async_computation | async-start | bytes 32768 | tf_op jit(solution)/shard_map/all_to_all | solution.py:147
  101.1 1.0 copy-start
  103.5 85.4 %copy-start.2 = (s32[1,1,2048]{2,1,0:T(1,128)S(1)}, s32[1,1,2048]{2,1,0:T(1,128)}, u32[]{:S(2)}) copy-start(s32[1,1,2048]{2,1,0:T(1,128)} %param.15) | copy-start | bytes 24580
  103.5 86.3 %copy-start.3 = (s32[1,1,2048]{2,1,0:T(1,128)S(1)}, s32[1,1,2048]{2,1,0:T(1,128)}, u32[]{:S(2)}) copy-start(s32[1,1,2048]{2,1,0:T(1,128)} %param.17) | copy-start | bytes 24580
  103.5 86.3 %copy-start.1 = (f32[1,1,2048]{2,1,0:T(1,128)S(1)}, f32[1,1,2048]{2,1,0:T(1,128)}, u32[]{:S(2)}) copy-start(f32[1,1,2048]{2,1,0:T(1,128)} %param.16) | copy-start | bytes 24580
  103.5 82.3 %all-to-all-start.1 = ((f32[4,24,32,128]{3,1,0,2:T(8,128)}), f32[4,24,32,128]{3,1,0,2:T(8,128)S(1)}, u32[]{:S(2)}, u32[]{:S(2)}) async-start(f32[4,24,32,128]{3,1,0,2:T(8,128)} %pad_maximum_fusion.9), calls=%async_computation.1 | async-start | bytes 3145728 | tf_op jit(solution)/shard_map/all_to_all | solution.py:157
  185.8 31.2 %collective-permute-start.1 = (f32[4,24,32,128]{3,1,0,2:T(8,128)S(1)}, f32[4,24,32,128]{3,1,0,2:T(8,128)S(1)}, u32[]{:S(2)}, u32[]{:S(2)}) collective-permute-start(f32[4,24,32,128]{3,1,0,2:T(8,128)S(1)} %all-to-all-done.1), channel_id=1, source_target_pairs={{0,256},{256,0},{1,257},{257,1},{2,258},{258,2},{3,259},{259,3},{4... | collective-permute-start | bytes 4718600 | tf_op jit(solution)/shard_map/ppermute | solution.py:19
  246.5 4.4 %collective-permute-start.2 = (f32[6,4,1,128]{3,2,1,0:T(1,128)S(1)}, f32[6,4,1,128]{3,2,1,0:T(1,128)S(1)}, u32[]{:S(2)}, u32[]{:S(2)}) collective-permute-start(f32[6,4,1,128]{3,2,1,0:T(1,128)S(1)} %get-tuple-element.12), channel_id=1, source_target_pairs={{32,0},{64,32},{96,64},{128,96},{160,128},{192,160},{224,192},{33,... | collective-permute-start | bytes 36872 | tf_op jit(solution)/shard_map/ppermute | solution.py:30
  247.8 3.9 collective-permute-start.3
  256.4 26.6 %collective-permute-start.5 = (f32[6,4,130,1]{2,1,3,0:T(4,128)S(1)}, f32[6,4,130,1]{2,1,3,0:T(4,128)S(1)}, u32[]{:S(2)}, u32[]{:S(2)}) collective-permute-start(f32[6,4,130,1]{2,1,3,0:T(4,128)S(1)} %copy.100), channel_id=1, source_target_pairs={{0,1},{1,2},{2,3},{3,4},{4,5},{5,6},{6,7},{7,8},{8,9},{9,10},{10,1... | collective-permute-start | bytes 37448 | tf_op jit(solution)/shard_map/ppermute | solution.py:29
  266.4 18.4 %collective-permute-start.4 = (f32[6,4,130,1]{2,1,3,0:T(4,128)S(1)}, f32[6,4,130,1]{2,1,3,0:T(4,128)S(1)}, u32[]{:S(2)}, u32[]{:S(2)}) collective-permute-start(f32[6,4,130,1]{2,1,3,0:T(4,128)S(1)} %copy.98), channel_id=1, source_target_pairs={{1,0},{2,1},{3,2},{4,3},{5,4},{6,5},{7,6},{8,7},{9,8},{10,9},{11,1... | collective-permute-start | bytes 37448 | tf_op jit(solution)/shard_map/ppermute | solution.py:30
  290.3 4.8 %collective-permute-start.6 = (f32[3,4,1,128]{3,2,1,0:T(1,128)S(1)}, f32[3,4,1,128]{3,2,1,0:T(1,128)S(1)}, u32[]{:S(2)}, u32[]{:S(2)}) collective-permute-start(f32[3,4,1,128]{3,2,1,0:T(1,128)S(1)} %get-tuple-element.10), channel_id=1, source_target_pairs={{32,0},{64,32},{96,64},{128,96},{160,128},{192,160},{224,192},{33,... | collective-permute-start | bytes 18440 | tf_op jit(solution)/shard_map/ppermute | solution.py:30
  291.6 4.3 %collective-permute-start.7 = (f32[3,4,1,128]{3,2,1,0:T(1,128)S(1)}, f32[3,4,1,128]{3,2,1,0:T(1,128)S(1)}, u32[]{:S(2)}, u32[]{:S(2)}) collective-permute-start(f32[3,4,1,128]{3,2,1,0:T(1,128)S(1)} %get-tuple-element.9), channel_id=1, source_target_pairs={{0,32},{32,64},{64,96},{96,128},{128,160},{160,192},{192,224},{1,3... | collective-permute-start | bytes 18440 | tf_op jit(solution)/shard_map/ppermute | solution.py:29
  299.0 9.0 %collective-permute-start.8 = (f32[3,4,130,1]{2,1,3,0:T(4,128)S(1)}, f32[3,4,130,1]{2,1,3,0:T(4,128)S(1)}, u32[]{:S(2)}, u32[]{:S(2)}) collective-permute-start(f32[3,4,130,1]{2,1,3,0:T(4,128)S(1)} %copy.103), channel_id=1, source_target_pairs={{1,0},{2,1},{3,2},{4,3},{5,4},{6,5},{7,6},{8,7},{9,8},{10,9},{11,1... | collective-permute-start | bytes 18728 | tf_op jit(solution)/shard_map/ppermute | solution.py:30
  305.8 8.0 %collective-permute-start.9 = (f32[3,4,130,1]{2,1,3,0:T(4,128)S(1)}, f32[3,4,130,1]{2,1,3,0:T(4,128)S(1)}, u32[]{:S(2)}, u32[]{:S(2)}) collective-permute-start(f32[3,4,130,1]{2,1,3,0:T(4,128)S(1)} %copy.105), channel_id=1, source_target_pairs={{0,1},{1,2},{2,3},{3,4},{4,5},{5,6},{6,7},{7,8},{8,9},{9,10},{10,1... | collective-permute-start | bytes 18728 | tf_op jit(solution)/shard_map/ppermute | solution.py:29
  316.4 5.2 %collective-permute-start.10 = (f32[4,1,128]{2,1,0:T(1,128)S(1)}, f32[4,1,128]{2,1,0:T(1,128)S(1)}, u32[]{:S(2)}, u32[]{:S(2)}) collective-permute-start(f32[4,1,128]{2,1,0:T(1,128)S(1)} %get-tuple-element.29), channel_id=1, source_target_pairs={{32,0},{64,32},{96,64},{128,96},{160,128},{192,160},{224,192},{33,... | collective-permute-start | bytes 6152 | tf_op jit(solution)/shard_map/ppermute | solution.py:30
  317.7 4.7 %collective-permute-start.11 = (f32[4,1,128]{2,1,0:T(1,128)S(1)}, f32[4,1,128]{2,1,0:T(1,128)S(1)}, u32[]{:S(2)}, u32[]{:S(2)}) collective-permute-start(f32[4,1,128]{2,1,0:T(1,128)S(1)} %get-tuple-element.28), channel_id=1, source_target_pairs={{0,32},{32,64},{64,96},{96,128},{128,160},{160,192},{192,224},{1,3... | collective-permute-start | bytes 6152 | tf_op jit(solution)/shard_map/ppermute | solution.py:29
  322.6 10.2 %collective-permute-start.12 = (f32[4,130,1]{2,1,0:T(8,128)S(1)}, f32[4,130,1]{2,1,0:T(8,128)S(1)}, u32[]{:S(2)}, u32[]{:S(2)}) collective-permute-start(f32[4,130,1]{2,1,0:T(8,128)S(1)} %get-tuple-element.23), channel_id=1, source_target_pairs={{1,0},{2,1},{3,2},{4,3},{5,4},{6,5},{7,6},{8,7},{9,8},{10,9},{11,1... | collective-permute-start | bytes 6248 | tf_op jit(solution)/shard_map/ppermute | solution.py:30
  325.0 11.8 %collective-permute-start.13 = (f32[4,130,1]{2,1,0:T(8,128)S(1)}, f32[4,130,1]{2,1,0:T(8,128)S(1)}, u32[]{:S(2)}, u32[]{:S(2)}) collective-permute-start(f32[4,130,1]{2,1,0:T(8,128)S(1)} %get-tuple-element.24), channel_id=1, source_target_pairs={{0,1},{1,2},{2,3},{3,4},{4,5},{5,6},{6,7},{7,8},{8,9},{9,10},{10,1... | collective-permute-start | bytes 6248 | tf_op jit(solution)/shard_map/ppermute | solution.py:29
  337.9 38.5 %all-to-all-start.2 = ((f32[256,4,1]{1,2,0:T(1,128)}), f32[256,4,1]{1,2,0:T(1,128)S(1)}, u32[]{:S(2)}, u32[]{:S(2)}) async-start(f32[256,4,1]{1,2,0:T(1,128)} %stack.44), calls=%async_computation.2 | async-start | bytes 262144 | tf_op jit(solution)/shard_map/all_to_all | solution.py:192
  379.0 4.5 %collective-permute-start.14 = (f32[4,1,128]{2,1,0:T(1,128)S(1)}, f32[4,1,128]{2,1,0:T(1,128)S(1)}, u32[]{:S(2)}, u32[]{:S(2)}) collective-permute-start(f32[4,1,128]{2,1,0:T(1,128)S(1)} %get-tuple-element.27), channel_id=1, source_target_pairs={{32,0},{64,32},{96,64},{128,96},{160,128},{192,160},{224,192},{33,... | collective-permute-start | bytes 6152 | tf_op jit(solution)/shard_map/ppermute | solution.py:30
  380.3 3.9 collective-permute-start.15
  384.3 18.3 %collective-permute-start.16 = (f32[4,130,1]{2,1,0:T(8,128)S(1)}, f32[4,130,1]{2,1,0:T(8,128)S(1)}, u32[]{:S(2)}, u32[]{:S(2)}) collective-permute-start(f32[4,130,1]{2,1,0:T(8,128)S(1)} %get-tuple-element.21), channel_id=1, source_target_pairs={{1,0},{2,1},{3,2},{4,3},{5,4},{6,5},{7,6},{8,7},{9,8},{10,9},{11,1... | collective-permute-start | bytes 6248 | tf_op jit(solution)/shard_map/ppermute | solution.py:30
  388.0 14.6 %collective-permute-start.17 = (f32[4,130,1]{2,1,0:T(8,128)S(1)}, f32[4,130,1]{2,1,0:T(8,128)S(1)}, u32[]{:S(2)}, u32[]{:S(2)}) collective-permute-start(f32[4,130,1]{2,1,0:T(8,128)S(1)} %get-tuple-element.22), channel_id=1, source_target_pairs={{0,1},{1,2},{2,3},{3,4},{4,5},{5,6},{6,7},{7,8},{8,9},{9,10},{10,1... | collective-permute-start | bytes 6248 | tf_op jit(solution)/shard_map/ppermute | solution.py:29
